TPU v7x, 32 devices: a whole 2x2x4 slice. The times are simulated.
32 devices in a mesh: groups: 2 (over y), pairs: 4 (over z), mp: 4 (over x, core).
Axes of the slice: x: 2, y: 2, z: 4, core: 2. Of those that a mesh axis runs over, the one named last changes fastest.
Arguments:
- tokens: bfloat16 [512, 768], P(('groups', 'pairs'), 'mp'), parts along dimension 0, may hold values from -6 to 6
- pair_list: int32 [16, 2], P(('groups', 'pairs')), parts along dimension 0, may hold values from 0 to 7, as said below
- confidence: float32 [16, 64], P(('groups', 'pairs')), parts along dimension 0, may hold values from 0.1 to 10
- gain_self: float32 [768], replicated, may hold values from 0.1 to 1.9
- gain_query: float32 [768], replicated, may hold values from 0.1 to 1.9
- gain_context: float32 [768], replicated, may hold values from 0.1 to 1.9
- gain_mlp: float32 [768], replicated, may hold values from 0.1 to 1.9
- self_qkv: bfloat16 [3, 768, 768], P(None, None, 'mp'), may hold values from -1 to 1
- self_out: bfloat16 [768, 768], P('mp'), may hold values from -0.21875 to 0.21875
- cross_query: bfloat16 [768, 768], P(None, 'mp'), may hold values from -1 to 1
- cross_kv: bfloat16 [2, 768, 768], P(None, None, 'mp'), may hold values from -1 to 1
- cross_out: bfloat16 [768, 768], P('mp'), may hold values from -0.21875 to 0.21875
- mlp_up: bfloat16 [768, 3072], P(None, 'mp'), may hold values from -0.21875 to 0.21875
- mlp_down: bfloat16 [3072, 768], P('mp'), may hold values from -0.109375 to 0.109375
Outputs:
- image_features: bfloat16 [512, 768], P(('groups', 'pairs'), 'mp'), parts along dimension 0
There are 2 independent parts, one for each index of `groups`. A program takes and returns all parts, laid end to end along the dimension named above; an argument that names none is the same for every part. Nothing has to cross between parts.
Inputs may be any that keep to these rules, and one draw needn't show every extreme that they name: `pair_list`: in each block of 2 consecutive pairs the 4 images named are distinct and have distinct owners, the owner of image i being i // 2; the images of each owner are named in exactly 4 blocks; some images are named by no pair.
All inputs are finite; a program needn't handle non-finite values.
Results may differ from a plain program's by a relative error of at most 0.012.
Values may be sent and summed in bfloat16 or wider, within the bound.
No kernel may reach another device: no remote copies, remote signals or barrier semaphores. Data moves between devices by JAX's collectives and lax.ppermute only.
A program may use at most 64 MiB of HBM per device.

v0:
```python
import jax
import jax.numpy as jnp
from jax import lax
from jax.sharding import PartitionSpec as P

HEAD = 64
TOKS = 32
EPSILON = 1e-06


def layer_norm(values, gain):
    center = values - jnp.mean(values, axis=-1, keepdims=True)
    spread = jnp.mean(center * center, axis=-1, keepdims=True)
    return (center * lax.rsqrt(spread + EPSILON) * gain).astype(jnp.bfloat16)


def attend(query, keys, values, views_n):
    rows_n, width = query.shape
    heads_n = width // HEAD
    qh = query.reshape(views_n, TOKS, heads_n, HEAD)
    kh = keys.reshape(views_n, TOKS, heads_n, HEAD)
    vh = values.reshape(views_n, TOKS, heads_n, HEAD)
    scores = jnp.einsum("vqhc,vkhc->vhqk", qh, kh, preferred_element_type=jnp.float32) * HEAD ** (
        -0.5
    )
    probs = jax.nn.softmax(scores, axis=-1).astype(jnp.bfloat16)
    mixed = jnp.einsum("vhqk,vkhc->vqhc", probs, vh, preferred_element_type=jnp.float32)
    return mixed.astype(jnp.bfloat16).reshape(rows_n, width)


def swap(values, pairs):
    return lax.ppermute(values, "mp", pairs)


def mp_pairs(bit):
    n = 4
    return [(i, i ^ bit) for i in range(n)]


def mp_allreduce(term):
    if lax.axis_size("mp") != 4:
        return lax.psum(term.astype(jnp.float32), "mp")
    core = lax.axis_index("mp") % 2
    rows_n = term.shape[0]
    halves = term.reshape(2, rows_n // 2, term.shape[1])
    keep = jnp.where(core == 0, halves[0], halves[1])
    send = jnp.where(core == 0, halves[1], halves[0])
    got = swap(send, mp_pairs(1))
    chip_sum = (keep.astype(jnp.float32) + got.astype(jnp.float32)).astype(jnp.bfloat16)
    other = swap(chip_sum, mp_pairs(2))
    total = chip_sum.astype(jnp.float32) + other.astype(jnp.float32)
    rest = swap(total, mp_pairs(1))
    first = jnp.where(core == 0, total, rest)
    second = jnp.where(core == 0, rest, total)
    return jnp.concatenate([first, second], axis=0)


def mp_reduce_cols(term):
    if lax.axis_size("mp") != 4:
        full = lax.psum(term.astype(jnp.float32), "mp")
        quarter = term.shape[1] // lax.axis_size("mp")
        return lax.dynamic_slice_in_dim(full, lax.axis_index("mp") * quarter, quarter, 1)
    index = lax.axis_index("mp")
    core = index % 2
    chip = index // 2
    rows_n, width = term.shape
    parts = term.reshape(rows_n, 2, 2, width // 4)
    keep = jnp.where(core == 0, parts[:, :, 0], parts[:, :, 1])
    send = jnp.where(core == 0, parts[:, :, 1], parts[:, :, 0])
    got = swap(send, mp_pairs(1))
    both = keep.astype(jnp.float32) + got.astype(jnp.float32)
    mine = jnp.where(chip == 0, both[:, 0], both[:, 1])
    theirs = jnp.where(chip == 0, both[:, 1], both[:, 0])
    other = swap(theirs, mp_pairs(2))
    return mine + other


def mp_gather_cols(part):
    if lax.axis_size("mp") != 4:
        return lax.all_gather(part, "mp", axis=2, tiled=True)
    index = lax.axis_index("mp")
    core = index % 2
    chip = index // 2
    got = swap(part, mp_pairs(1))
    pair = jnp.where(
        core == 0, jnp.concatenate([part, got], axis=2), jnp.concatenate([got, part], axis=2)
    )
    other = swap(pair, mp_pairs(2))
    return jnp.where(
        chip == 0, jnp.concatenate([pair, other], axis=2), jnp.concatenate([other, pair], axis=2)
    )


def per_device(
    tokens,
    pair_list,
    confidence,
    gain_self,
    gain_query,
    gain_context,
    gain_mlp,
    self_qkv,
    self_out,
    cross_query,
    cross_kv,
    cross_out,
    mlp_up,
    mlp_down,
):
    quarter = tokens.shape[1]
    img_dev = tokens.shape[0] // TOKS
    pair_dev = pair_list.shape[0]
    views_n = 2 * pair_dev
    owners_n = lax.axis_size("pairs")
    every = lax.all_gather(tokens, "pairs", axis=0, tiled=True).reshape(
        owners_n * img_dev, TOKS, quarter
    )
    ids = pair_list.reshape(views_n)
    slices = jnp.take(every, ids, axis=0)
    start = mp_gather_cols(slices)
    width = start.shape[2]
    rows_n = views_n * TOKS
    flipped = start.reshape(pair_dev, 2, TOKS, width)
    flipped = jnp.concatenate([flipped[:, 1:], flipped[:, :1]], axis=1)
    begin = start.astype(jnp.float32).reshape(rows_n, width)
    context = layer_norm(flipped.astype(jnp.float32), gain_context).reshape(rows_n, width)
    normed = layer_norm(begin, gain_self)
    qkv = jnp.einsum("rd,kdc->krc", normed, self_qkv, preferred_element_type=jnp.float32).astype(
        jnp.bfloat16
    )
    term = jnp.dot(
        attend(qkv[0], qkv[1], qkv[2], views_n), self_out, preferred_element_type=jnp.float32
    )
    resid = begin + mp_allreduce(term.astype(jnp.bfloat16))
    normed = layer_norm(resid, gain_query)
    query = jnp.dot(normed, cross_query, preferred_element_type=jnp.float32).astype(jnp.bfloat16)
    keyval = jnp.einsum(
        "rd,kdc->krc", context, cross_kv, preferred_element_type=jnp.float32
    ).astype(jnp.bfloat16)
    term = jnp.dot(
        attend(query, keyval[0], keyval[1], views_n), cross_out, preferred_element_type=jnp.float32
    )
    resid = resid + mp_allreduce(term.astype(jnp.bfloat16))
    normed = layer_norm(resid, gain_mlp)
    hidden = jax.nn.gelu(
        jnp.dot(normed, mlp_up, preferred_element_type=jnp.float32), approximate=False
    )
    term = jnp.dot(hidden.astype(jnp.bfloat16), mlp_down, preferred_element_type=jnp.float32)
    offset = lax.axis_index("mp") * quarter
    final = lax.dynamic_slice_in_dim(resid, offset, quarter, 1) + mp_reduce_cols(
        term.astype(jnp.bfloat16)
    )
    conf = confidence.reshape(views_n, TOKS)
    weighted = (final.reshape(views_n, TOKS, quarter) * conf[:, :, None]).reshape(
        views_n, TOKS * quarter
    )
    source = ids // img_dev
    slot = (ids % img_dev + 1).astype(jnp.float32)
    route = (source[None, :] == jnp.arange(owners_n)[:, None]).astype(jnp.float32)
    back = jnp.dot(route, weighted, precision=lax.Precision.HIGHEST)
    back_weight = jnp.dot(route, conf, precision=lax.Precision.HIGHEST)
    back_slot = jnp.dot(route, slot[:, None], precision=lax.Precision.HIGHEST)
    pad = jnp.zeros((owners_n, 128 - TOKS - 1), jnp.float32)
    payload = jnp.concatenate([back, back_weight, back_slot, pad], axis=1).astype(jnp.bfloat16)
    got = lax.all_to_all(payload, "pairs", split_axis=0, concat_axis=0, tiled=True).astype(
        jnp.float32
    )
    feat = got[:, : TOKS * quarter].reshape(owners_n, TOKS, quarter)
    got_weight = got[:, TOKS * quarter : TOKS * quarter + TOKS]
    got_slot = got[:, TOKS * quarter + TOKS]
    owner_match = (
        got_slot[None, :] == (jnp.arange(img_dev) + 1)[:, None].astype(jnp.float32)
    ).astype(jnp.float32)
    numer = jnp.einsum("ij,jtc->itc", owner_match, feat, precision=lax.Precision.HIGHEST)
    denom = jnp.dot(owner_match, got_weight, precision=lax.Precision.HIGHEST)
    result = numer / jnp.maximum(denom, 1.0)[:, :, None]
    return result.astype(jnp.bfloat16).reshape(img_dev * TOKS, quarter)


def solution(mesh):
    return jax.shard_map(
        per_device,
        mesh=mesh,
        in_specs=(
            P(("groups", "pairs"), "mp"),
            P(("groups", "pairs"), None),
            P(("groups", "pairs"), None),
            P(),
            P(),
            P(),
            P(),
            P(None, None, "mp"),
            P("mp", None),
            P(None, "mp"),
            P(None, None, "mp"),
            P("mp", None),
            P(None, "mp"),
            P("mp", None),
        ),
        out_specs=P(("groups", "pairs"), "mp"),
        check_vma=False,
    )
```

profile of v0, /device:TPU:0, one launch (start us, length us, event | category | flops | bytes accessed | tf_op | source)
XLA Modules:
  0.0 69.1 jit_solution(16886699572011220582)
XLA Ops:
  0.0 0.9 %reshape.280 = s32[4,1]{0,1:T(1,128)S(1)} reshape(s32[2,2]{1,0:T(2,128)} %param.15) | data formatting | bytes 32 | tf_op jit(solution)/shard_map/reshape | solution.py:118
  0.9 0.8 %reshape.278 = s32[4]{0:T(128)S(1)} reshape(s32[2,2]{1,0:T(2,128)} %param.15) | data formatting | bytes 32 | tf_op jit(solution)/shard_map/reshape | solution.py:118
  1.6 15.3 %all_gather.3 = bf16[256,192]{1,0:T(8,128)(2,1)S(1)} all-gather(bf16[64,192]{1,0:T(8,128)(2,1)} %param.14), channel_id=1, replica_groups=mesh['groups'=2,'pairs'=4,'mp'=4] {'pairs'}, dimensions={0}, use_global_device_ids=true | all-gather | bytes 122880 | tf_op jit(solution)/shard_map/all_gather | solution.py:115
  16.9 0.6 gather_fusion
  17.6 0.7 compare_and_fusion
  18.9 1.6 %collective-permute-start.1 = (bf16[4,32,384]{2,1,0:T(8,128)(2,1)S(1)}, bf16[4,32,384]{2,1,0:T(8,128)(2,1)S(1)}, u32[]{:S(2)}, u32[]{:S(2)}) collective-permute-start(bf16[4,32,384]{2,1,0:T(8,128)(2,1)S(1)} %maximum_select_fusion.3), channel_id=1, source_target_pairs={{0,2},{1,3},{2,0},{3,1},{4,6},{5,7},{6,4},{7,5},{8,10},{9,11},{10,... | collective-permute-start | bytes 294920 | tf_op jit(solution)/shard_map/ppermute | solution.py:32
  20.7 3.2 %collective-permute-done.1 = bf16[4,32,384]{2,1,0:T(8,128)(2,1)S(1)} collective-permute-done((bf16[4,32,384]{2,1,0:T(8,128)(2,1)S(1)}, bf16[4,32,384]{2,1,0:T(8,128)(2,1)S(1)}, u32[]{:S(2)}, u32[]{:S(2)}) %collective-permute-start.1) | collective-permute-done | bytes 98336 | tf_op jit(solution)/shard_map/ppermute | solution.py:32
  24.9 0.5 fusion.33
  26.2 0.3 fusion.7
  27.3 0.3 copy-done.1
  27.6 0.3 fusion.149
  27.9 0.5 collective-permute-done.2
  28.5 1.6 %collective-permute-start.3 = (bf16[64,768]{1,0:T(8,128)(2,1)S(1)}, bf16[64,768]{1,0:T(8,128)(2,1)S(1)}, u32[]{:S(2)}, u32[]{:S(2)}) collective-permute-start(bf16[64,768]{1,0:T(8,128)(2,1)S(1)} %add_convert_fusion.1), channel_id=1, source_target_pairs={{0,2},{1,3},{2,0},{3,1},{4,6},{5,7},{6,4},{7,5},{8,10},{9,11},{10,... | collective-permute-start | bytes 294920 | tf_op jit(solution)/shard_map/ppermute | solution.py:32
  30.1 3.3 %collective-permute-done.3 = bf16[64,768]{1,0:T(8,128)(2,1)S(1)} collective-permute-done((bf16[64,768]{1,0:T(8,128)(2,1)S(1)}, bf16[64,768]{1,0:T(8,128)(2,1)S(1)}, u32[]{:S(2)}, u32[]{:S(2)}) %collective-permute-start.3) | collective-permute-done | bytes 98336 | tf_op jit(solution)/shard_map/ppermute | solution.py:32
  33.8 1.1 %collective-permute-done.4 = f32[64,768]{1,0:T(8,128)S(1)} collective-permute-done((f32[64,768]{1,0:T(8,128)S(1)}, f32[64,768]{1,0:T(8,128)S(1)}, u32[]{:S(2)}, u32[]{:S(2)}) %collective-permute-start.4) | collective-permute-done | bytes 196640 | tf_op jit(solution)/shard_map/ppermute | solution.py:32
  35.4 0.3 convolution_convert_fusion.6
  35.8 0.2 convolution_multiply_fusion
  36.2 0.3 fusion.8
  37.2 1.2 %collective-permute-done.5 = bf16[64,768]{1,0:T(8,128)(2,1)S(1)} collective-permute-done((bf16[64,768]{1,0:T(8,128)(2,1)S(1)}, bf16[64,768]{1,0:T(8,128)(2,1)S(1)}, u32[]{:S(2)}, u32[]{:S(2)}) %collective-permute-start.5) | collective-permute-done | bytes 98336 | tf_op jit(solution)/shard_map/ppermute | solution.py:32
  38.4 1.6 %collective-permute-start.6 = (bf16[64,768]{1,0:T(8,128)(2,1)S(1)}, bf16[64,768]{1,0:T(8,128)(2,1)S(1)}, u32[]{:S(2)}, u32[]{:S(2)}) collective-permute-start(bf16[64,768]{1,0:T(8,128)(2,1)S(1)} %add_convert_fusion), channel_id=1, source_target_pairs={{0,2},{1,3},{2,0},{3,1},{4,6},{5,7},{6,4},{7,5},{8,10},{9,11},{10,... | collective-permute-start | bytes 294920 | tf_op jit(solution)/shard_map/ppermute | solution.py:32
  40.3 3.1 %collective-permute-done.6 = bf16[64,768]{1,0:T(8,128)(2,1)S(1)} collective-permute-done((bf16[64,768]{1,0:T(8,128)(2,1)S(1)}, bf16[64,768]{1,0:T(8,128)(2,1)S(1)}, u32[]{:S(2)}, u32[]{:S(2)}) %collective-permute-start.6) | collective-permute-done | bytes 98336 | tf_op jit(solution)/shard_map/ppermute | solution.py:32
  43.5 1.4 %collective-permute-done.7 = f32[64,768]{1,0:T(8,128)S(1)} collective-permute-done((f32[64,768]{1,0:T(8,128)S(1)}, f32[64,768]{1,0:T(8,128)S(1)}, u32[]{:S(2)}, u32[]{:S(2)}) %collective-permute-start.7) | collective-permute-done | bytes 196640 | tf_op jit(solution)/shard_map/ppermute | solution.py:32
  45.3 1.5 %convolution_convert_fusion.1 = bf16[128,768]{1,0:T(8,128)(2,1)S(1)} fusion(bf16[768,768]{1,0:T(8,128)(2,1)S(1)} %copy-done, bf16[768,768]{1,0:T(8,128)(2,1)S(1)} %copy-done.6, f32[128,768]{1,0:T(8,128)S(1)} %get-tuple-element.6, f32[768]{0:T(1024)S(1)} %copy-done.11, f32[128]{0:T(128)S(1)} %add_rsqrt_fusion.1, f32[128]{0:T(128)S(1)} %broadcast_multiply_fusion.1), kind=kOutput, calls=%fused_computation.7 | convolution fusion | flops 308871168 | bytes 2953216 | tf_op jit(solution)/shard_map/dot_general | solution.py:148
  47.7 1.0 %collective-permute-done.8 = bf16[128,2,192]{2,0,1:T(8,128)(2,1)S(1)} collective-permute-done((bf16[128,2,192]{2,0,1:T(8,128)(2,1)S(1)}, bf16[128,2,192]{2,0,1:T(8,128)(2,1)S(1)}, u32[]{:S(2)}, u32[]{:S(2)}) %collective-permute-start.8) | collective-permute-done | bytes 98336 | tf_op jit(solution)/shard_map/ppermute | solution.py:32
  48.7 1.6 %collective-permute-start.9 = (f32[128,192]{1,0:T(8,128)S(1)}, f32[128,192]{1,0:T(8,128)S(1)}, u32[]{:S(2)}, u32[]{:S(2)}) collective-permute-start(f32[128,192]{1,0:T(8,128)S(1)} %select_bitcast_fusion), channel_id=1, source_target_pairs={{0,2},{1,3},{2,0},{3,1},{4,6},{5,7},{6,4},{7,5},{8,10},{9,11},{10,... | collective-permute-start | bytes 294920 | tf_op jit(solution)/shard_map/ppermute | solution.py:32
  50.4 3.9 %collective-permute-done.9 = f32[128,192]{1,0:T(8,128)S(1)} collective-permute-done((f32[128,192]{1,0:T(8,128)S(1)}, f32[128,192]{1,0:T(8,128)S(1)}, u32[]{:S(2)}, u32[]{:S(2)}) %collective-permute-start.9) | collective-permute-done | bytes 98336 | tf_op jit(solution)/shard_map/ppermute | solution.py:32
  54.9 0.5 broadcast.282
  55.4 0.7 reduce.2
  56.1 0.7 %reshape.313 = bf16[4,2,3136]{2,1,0:T(2,128)(2,1)} reshape(bf16[4,6272]{1,0:T(4,128)(2,1)S(1)} %reduce.2) | data formatting | bytes 100352
  56.8 5.0 %all-to-all-start = ((bf16[4,2,3136]{2,1,0:T(2,128)(2,1)}), bf16[4,2,3136]{2,1,0:T(2,128)(2,1)S(1)}, u32[]{:S(2)}, u32[]{:S(2)}) async-start(bf16[4,2,3136]{2,1,0:T(2,128)(2,1)} %reshape.313), calls=%async_computation | async-start | bytes 102400 | tf_op jit(solution)/shard_map/all_to_all | solution.py:165
  61.8 5.7 %all-to-all-done = bf16[4,2,3136]{2,1,0:T(2,128)(2,1)S(1)} async-done(((bf16[4,2,3136]{2,1,0:T(2,128)(2,1)}), bf16[4,2,3136]{2,1,0:T(2,128)(2,1)S(1)}, u32[]{:S(2)}, u32[]{:S(2)}) %all-to-all-start) | async-done | bytes 50208 | tf_op jit(solution)/shard_map/all_to_all | solution.py:165
  68.5 0.6 copy.95
  (118 shorter events, 8.6 us)
Async XLA Ops:
  0.0 45.3 %copy-start = (bf16[768,768]{1,0:T(8,128)(2,1)S(1)}, bf16[768,768]{1,0:T(8,128)(2,1)}, u32[]{:S(2)}) copy-start(bf16[768,768]{1,0:T(8,128)(2,1)} %param.27) | copy-start | bytes 3538948
  17.5 1.3 %collective-permute-start = (bf16[4,32,192]{2,1,0:T(8,128)(2,1)S(1)}, bf16[4,32,192]{2,1,0:T(8,128)(2,1)S(1)}, u32[]{:S(2)}, u32[]{:S(2)}) collective-permute-start(bf16[4,32,192]{2,1,0:T(8,128)(2,1)S(1)} %broadcast_select_fusion.6), channel_id=1, source_target_pairs={{0,1},{1,0},{2,3},{3,2},{4,5},{5,4},{6,7},{7,6},{8,9},{9,8},{10,11... | collective-permute-start | bytes 147464 | tf_op jit(solution)/shard_map/ppermute | solution.py:32
  18.9 5.1 %collective-permute-start.1 = (bf16[4,32,384]{2,1,0:T(8,128)(2,1)S(1)}, bf16[4,32,384]{2,1,0:T(8,128)(2,1)S(1)}, u32[]{:S(2)}, u32[]{:S(2)}) collective-permute-start(bf16[4,32,384]{2,1,0:T(8,128)(2,1)S(1)} %maximum_select_fusion.3), channel_id=1, source_target_pairs={{0,2},{1,3},{2,0},{3,1},{4,6},{5,7},{6,4},{7,5},{8,10},{9,11},{10,... | collective-permute-start | bytes 294920 | tf_op jit(solution)/shard_map/ppermute | solution.py:32
  20.6 4.3 %copy-start.7 = (bf16[3,768,192]{1,2,0:T(8,128)(2,1)S(1)}, bf16[3,768,192]{1,2,0:T(8,128)(2,1)}, u32[]{:S(2)}) copy-start(bf16[3,768,192]{1,2,0:T(8,128)(2,1)} %param.21) | copy-start | bytes 2654212
  20.6 4.3 %copy-start.9 = (f32[768]{0:T(1024)S(1)}, f32[768]{0:T(1024)}, u32[]{:S(2)}) copy-start(f32[768]{0:T(1024)} %param.17) | copy-start | bytes 9220
  25.9 1.0 %copy-start.2 = (bf16[192,768]{1,0:T(8,128)(2,1)S(1)}, bf16[192,768]{1,0:T(8,128)(2,1)}, u32[]{:S(2)}) copy-start(bf16[192,768]{1,0:T(8,128)(2,1)} %param.22) | copy-start | bytes 884740
  26.2 1.0 %copy-start.4 = (f32[768]{0:T(1024)S(1)}, f32[768]{0:T(1024)}, u32[]{:S(2)}) copy-start(f32[768]{0:T(1024)} %param.19) | copy-start | bytes 9220
  26.5 1.1 %copy-start.1 = (bf16[2,768,192]{1,2,0:T(8,128)(2,1)S(1)}, bf16[2,768,192]{1,2,0:T(8,128)(2,1)}, u32[]{:S(2)}) copy-start(bf16[2,768,192]{1,2,0:T(8,128)(2,1)} %param.24) | copy-start | bytes 1769476
  27.1 1.4 %collective-permute-start.2 = (bf16[64,768]{1,0:T(8,128)(2,1)S(1)}, bf16[64,768]{1,0:T(8,128)(2,1)S(1)}, u32[]{:S(2)}, u32[]{:S(2)}) collective-permute-start(bf16[64,768]{1,0:T(8,128)(2,1)S(1)} %broadcast_select_fusion.5), channel_id=1, source_target_pairs={{0,1},{1,0},{2,3},{3,2},{4,5},{5,4},{6,7},{7,6},{8,9},{9,8},{10,11... | collective-permute-start | bytes 294920 | tf_op jit(solution)/shard_map/ppermute | solution.py:32
  28.5 4.9 %collective-permute-start.3 = (bf16[64,768]{1,0:T(8,128)(2,1)S(1)}, bf16[64,768]{1,0:T(8,128)(2,1)S(1)}, u32[]{:S(2)}, u32[]{:S(2)}) collective-permute-start(bf16[64,768]{1,0:T(8,128)(2,1)S(1)} %add_convert_fusion.1), channel_id=1, source_target_pairs={{0,2},{1,3},{2,0},{3,1},{4,6},{5,7},{6,4},{7,5},{8,10},{9,11},{10,... | collective-permute-start | bytes 294920 | tf_op jit(solution)/shard_map/ppermute | solution.py:32
  33.4 1.5 %collective-permute-start.4 = (f32[64,768]{1,0:T(8,128)S(1)}, f32[64,768]{1,0:T(8,128)S(1)}, u32[]{:S(2)}, u32[]{:S(2)}) collective-permute-start(f32[64,768]{1,0:T(8,128)S(1)} %convert_add_fusion.3), channel_id=1, source_target_pairs={{0,1},{1,0},{2,3},{3,2},{4,5},{5,4},{6,7},{7,6},{8,9},{9,8},{10,11... | collective-permute-start | bytes 589832 | tf_op jit(solution)/shard_map/ppermute | solution.py:32
  33.5 1.8 %copy-start.8 = (bf16[768,192]{0,1:T(8,128)(2,1)S(1)}, bf16[768,192]{0,1:T(8,128)(2,1)}, u32[]{:S(2)}) copy-start(bf16[768,192]{0,1:T(8,128)(2,1)} %param.23) | copy-start | bytes 884740
  33.5 1.8 %copy-start.10 = (f32[768]{0:T(1024)S(1)}, f32[768]{0:T(1024)}, u32[]{:S(2)}) copy-start(f32[768]{0:T(1024)} %param.18) | copy-start | bytes 9220
  35.8 1.0 %copy-start.3 = (bf16[192,768]{1,0:T(8,128)(2,1)S(1)}, bf16[192,768]{1,0:T(8,128)(2,1)}, u32[]{:S(2)}) copy-start(bf16[192,768]{1,0:T(8,128)(2,1)} %param.25) | copy-start | bytes 884740
  36.1 3.8 %copy-start.5 = (f32[2,64]{1,0:T(2,128)S(1)}, f32[2,64]{1,0:T(2,128)}, u32[]{:S(2)}) copy-start(f32[2,64]{1,0:T(2,128)} %param.16) | copy-start | bytes 1540
  37.0 1.4 %collective-permute-start.5 = (bf16[64,768]{1,0:T(8,128)(2,1)S(1)}, bf16[64,768]{1,0:T(8,128)(2,1)S(1)}, u32[]{:S(2)}, u32[]{:S(2)}) collective-permute-start(bf16[64,768]{1,0:T(8,128)(2,1)S(1)} %broadcast_select_fusion.2), channel_id=1, source_target_pairs={{0,1},{1,0},{2,3},{3,2},{4,5},{5,4},{6,7},{7,6},{8,9},{9,8},{10,11... | collective-permute-start | bytes 294920 | tf_op jit(solution)/shard_map/ppermute | solution.py:32
  38.4 4.9 %collective-permute-start.6 = (bf16[64,768]{1,0:T(8,128)(2,1)S(1)}, bf16[64,768]{1,0:T(8,128)(2,1)S(1)}, u32[]{:S(2)}, u32[]{:S(2)}) collective-permute-start(bf16[64,768]{1,0:T(8,128)(2,1)S(1)} %add_convert_fusion), channel_id=1, source_target_pairs={{0,2},{1,3},{2,0},{3,1},{4,6},{5,7},{6,4},{7,5},{8,10},{9,11},{10,... | collective-permute-start | bytes 294920 | tf_op jit(solution)/shard_map/ppermute | solution.py:32
  43.4 1.5 %collective-permute-start.7 = (f32[64,768]{1,0:T(8,128)S(1)}, f32[64,768]{1,0:T(8,128)S(1)}, u32[]{:S(2)}, u32[]{:S(2)}) collective-permute-start(f32[64,768]{1,0:T(8,128)S(1)} %convert_add_fusion.2), channel_id=1, source_target_pairs={{0,1},{1,0},{2,3},{3,2},{4,5},{5,4},{6,7},{7,6},{8,9},{9,8},{10,11... | collective-permute-start | bytes 589832 | tf_op jit(solution)/shard_map/ppermute | solution.py:32
  43.5 1.8 %copy-start.6 = (bf16[768,768]{1,0:T(8,128)(2,1)S(1)}, bf16[768,768]{1,0:T(8,128)(2,1)}, u32[]{:S(2)}) copy-start(bf16[768,768]{1,0:T(8,128)(2,1)} %param.26) | copy-start | bytes 3538948
  43.5 1.8 %copy-start.11 = (f32[768]{0:T(1024)S(1)}, f32[768]{0:T(1024)}, u32[]{:S(2)}) copy-start(f32[768]{0:T(1024)} %param.20) | copy-start | bytes 9220
  47.2 1.4 %collective-permute-start.8 = (bf16[128,2,192]{2,0,1:T(8,128)(2,1)S(1)}, bf16[128,2,192]{2,0,1:T(8,128)(2,1)S(1)}, u32[]{:S(2)}, u32[]{:S(2)}) collective-permute-start(bf16[128,2,192]{2,0,1:T(8,128)(2,1)S(1)} %select_bitcast_fusion.1), channel_id=1, source_target_pairs={{0,1},{1,0},{2,3},{3,2},{4,5},{5,4},{6,7},{7,6},{8,9},{9,8},{10,11... | collective-permute-start | bytes 294920 | tf_op jit(solution)/shard_map/ppermute | solution.py:32
  48.7 5.6 %collective-permute-start.9 = (f32[128,192]{1,0:T(8,128)S(1)}, f32[128,192]{1,0:T(8,128)S(1)}, u32[]{:S(2)}, u32[]{:S(2)}) collective-permute-start(f32[128,192]{1,0:T(8,128)S(1)} %select_bitcast_fusion), channel_id=1, source_target_pairs={{0,2},{1,3},{2,0},{3,1},{4,6},{5,7},{6,4},{7,5},{8,10},{9,11},{10,... | collective-permute-start | bytes 294920 | tf_op jit(solution)/shard_map/ppermute | solution.py:32
  56.8 10.7 %all-to-all-start = ((bf16[4,2,3136]{2,1,0:T(2,128)(2,1)}), bf16[4,2,3136]{2,1,0:T(2,128)(2,1)S(1)}, u32[]{:S(2)}, u32[]{:S(2)}) async-start(bf16[4,2,3136]{2,1,0:T(2,128)(2,1)} %reshape.313), calls=%async_computation | async-start | bytes 102400 | tf_op jit(solution)/shard_map/all_to_all | solution.py:165
where the time goes:
time: 69.4 us; the launch traced here: 69.1 us
  waiting for transfers between devices  24.7 us (36%)
  blocking collectives  15.3 us (22%)
  starting transfers between devices  11.8 us (17%)
  local copies, waits for them, and re-layouts  7.6 us (11%)
  matrix products  4.83 us (7%)
  other arithmetic  4.32 us (6%)
    ppermute x10, waiting for transfers between devices, swap(): return lax.ppermute(values, 'mp', pairs)  19 us
    all_gather x1, blocking collectives, per_device(): lax.all_gather(tokens, 'pairs', axis=0, tiled=True)  15.3 us
    ppermute x10, starting transfers between devices, swap(): return lax.ppermute(values, 'mp', pairs)  6.86 us
    all_to_all x1, waiting for transfers between devices, per_device(): lax.all_to_all(payload, 'pairs', split_axis=0, concat_axis=0, tiled=True)  5.7 us
    all_to_all x1, starting transfers between devices, per_device(): lax.all_to_all(payload, 'pairs', split_axis=0, concat_axis=0, tiled=True)  4.97 us
    unnamed x29, local copies, waits for them, and re-layouts  1.71 us
    reshape x2, local copies, waits for them, and re-layouts, per_device(): ids = pair_list.reshape(views_n)  1.61 us
    dot_general x1, matrix products, per_device(): jnp.dot(hidden.astype(jnp.bfloat16), mlp_down, preferred_element_type=jnp...  1.45 us
  transfers between devices with their start and end apart: 11, of which 11 were waited for; matrix products, arithmetic and copies ran while one was open for 4% of the time, Pallas kernels for 0%

commit v1 on v0

--- a/solution.py
+++ b/solution.py
@@ -6,6 +6,29 @@
 HEAD = 64
 TOKS = 32
 EPSILON = 1e-06
+
+
+def in_blocks(value, dim, count):
+    shape = value.shape
+    blocks = value.reshape(*shape[:dim], count, shape[dim] // count, *shape[dim + 1 :])
+    return jnp.moveaxis(blocks, dim, 0)
+
+
+def laid_out(blocks, dim):
+    shape = list(blocks.shape[1:])
+    shape[dim] *= blocks.shape[0]
+    return jnp.moveaxis(blocks, 0, dim).reshape(shape)
+
+
+def swapped_with_each(shard, axis, split_dim, concat_dim):
+    count, index = (lax.axis_size(axis), lax.axis_index(axis))
+    pieces = in_blocks(shard, split_dim, count)
+    outs = [pieces[index]]
+    for hop in range(1, count):
+        sent = pieces[index ^ hop]
+        outs.append(lax.ppermute(sent, axis, [(i, i ^ hop) for i in range(count)]))
+    pieces = jnp.stack(outs)[index ^ jnp.arange(count)]
+    return laid_out(pieces, concat_dim)
 
 
 def layer_norm(values, gain):
@@ -162,9 +185,7 @@
     back_slot = jnp.dot(route, slot[:, None], precision=lax.Precision.HIGHEST)
     pad = jnp.zeros((owners_n, 128 - TOKS - 1), jnp.float32)
     payload = jnp.concatenate([back, back_weight, back_slot, pad], axis=1).astype(jnp.bfloat16)
-    got = lax.all_to_all(payload, "pairs", split_axis=0, concat_axis=0, tiled=True).astype(
-        jnp.float32
-    )
+    got = swapped_with_each(payload, "pairs", 0, 0).astype(jnp.float32)
     feat = got[:, : TOKS * quarter].reshape(owners_n, TOKS, quarter)
     got_weight = got[:, TOKS * quarter : TOKS * quarter + TOKS]
     got_slot = got[:, TOKS * quarter + TOKS]

time: 69.4 us -> 65.9 us (0.950)
  waiting for transfers between devices: 24.7 us -> 23 us
    all_to_all x1 -> x0, waiting for transfers between devices: 5.7 us -> none  [per_device(): lax.all_to_all(payload, 'pairs', split_axis=0, concat_axis=0, tiled=True)]
    all_to_all x1 -> x0, starting transfers between devices: 4.97 us -> none  [per_device(): lax.all_to_all(payload, 'pairs', split_axis=0, concat_axis=0, tiled=True)]
    ppermute x0 -> x3, starting transfers between devices: none -> 4.45 us  [swapped_with_each(): outs.append(lax.ppermute(sent, axis, [(i, i ^ hop) for i in range(count)]))]
    ppermute x0 -> x3, waiting for transfers between devices: none -> 4.04 us  [swapped_with_each(): outs.append(lax.ppermute(sent, axis, [(i, i ^ hop) for i in range(count)]))]
    unnamed x29 -> x26, local copies, waits for them, and re-layouts: 1.71 us -> 0.82 us
  transfers between devices with their start and end apart: 11 -> 13, of which waited for: 11 -> 12; matrix products, arithmetic and copies ran while one was open for 4% -> 4% of each run, Pallas kernels for 0% -> 0%
where the time goes in v1:
time: 65.9 us; the launch traced here: 65.7 us
  waiting for transfers between devices  23 us (35%)
  blocking collectives  15.3 us (23%)
  starting transfers between devices  11.3 us (17%)
  local copies, waits for them, and re-layouts  6.91 us (10%)
  matrix products  4.83 us (7%)
  other arithmetic  3.8 us (6%)
    ppermute x10, waiting for transfers between devices, swap(): return lax.ppermute(values, 'mp', pairs)  19 us
    all_gather x1, blocking collectives, per_device(): lax.all_gather(tokens, 'pairs', axis=0, tiled=True)  15.3 us
    ppermute x10, starting transfers between devices, swap(): return lax.ppermute(values, 'mp', pairs)  6.86 us
    ppermute x3, starting transfers between devices, swapped_with_each(): outs.append(lax.ppermute(sent, axis, [(i, i ^ hop) for i in range(count)]))  4.45 us
    ppermute x3, waiting for transfers between devices, swapped_with_each(): outs.append(lax.ppermute(sent, axis, [(i, i ^ hop) for i in range(count)]))  4.04 us
    reshape x2, local copies, waits for them, and re-layouts, per_device(): ids = pair_list.reshape(views_n)  1.61 us
    dot_general x1, matrix products, per_device(): jnp.dot(hidden.astype(jnp.bfloat16), mlp_down, preferred_element_type=jnp...  1.45 us
  transfers between devices with their start and end apart: 13, of which 12 were waited for; matrix products, arithmetic and copies ran while one was open for 4% of the time, Pallas kernels for 0%

profile of v1, /device:TPU:0, one launch (start us, length us, event | category | flops | bytes accessed | tf_op | source)
XLA Modules:
  0.0 65.7 jit_solution(18272050686934378141)
XLA Ops:
  0.0 0.9 %reshape.253 = s32[4,1]{0,1:T(1,128)S(1)} reshape(s32[2,2]{1,0:T(2,128)} %param.15) | data formatting | bytes 32 | tf_op jit(solution)/shard_map/reshape | solution.py:141
  0.9 0.8 %reshape.251 = s32[4]{0:T(128)S(1)} reshape(s32[2,2]{1,0:T(2,128)} %param.15) | data formatting | bytes 32 | tf_op jit(solution)/shard_map/reshape | solution.py:141
  1.6 15.3 %all_gather.3 = bf16[256,192]{1,0:T(8,128)(2,1)S(1)} all-gather(bf16[64,192]{1,0:T(8,128)(2,1)} %param.14), channel_id=1, replica_groups=mesh['groups'=2,'pairs'=4,'mp'=4] {'pairs'}, dimensions={0}, use_global_device_ids=true | all-gather | bytes 122880 | tf_op jit(solution)/shard_map/all_gather | solution.py:138
  16.9 0.6 gather_fusion
  17.6 0.7 %compare_and_fusion = pred[2,2]{1,0:T(4,128)(4,1)S(1)} fusion(s32[2,2]{1,0:T(2,128)} %param.15), kind=kLoop, calls=%fused_computation.156 | loop fusion | flops 24 | bytes 20 | tf_op jit(solution)/shard_map/jit(_take)/and | solution.py:142
  18.9 1.6 %collective-permute-start.1 = (bf16[4,32,384]{2,1,0:T(8,128)(2,1)S(1)}, bf16[4,32,384]{2,1,0:T(8,128)(2,1)S(1)}, u32[]{:S(2)}, u32[]{:S(2)}) collective-permute-start(bf16[4,32,384]{2,1,0:T(8,128)(2,1)S(1)} %maximum_select_fusion.3), channel_id=1, source_target_pairs={{0,2},{1,3},{2,0},{3,1},{4,6},{5,7},{6,4},{7,5},{8,10},{9,11},{10,... | collective-permute-start | bytes 294920 | tf_op jit(solution)/shard_map/ppermute | solution.py:55
  20.7 3.2 %collective-permute-done.1 = bf16[4,32,384]{2,1,0:T(8,128)(2,1)S(1)} collective-permute-done((bf16[4,32,384]{2,1,0:T(8,128)(2,1)S(1)}, bf16[4,32,384]{2,1,0:T(8,128)(2,1)S(1)}, u32[]{:S(2)}, u32[]{:S(2)}) %collective-permute-start.1) | collective-permute-done | bytes 98336 | tf_op jit(solution)/shard_map/ppermute | solution.py:55
  24.9 0.5 fusion.31
  25.9 0.2 convolution_multiply_fusion.1
  26.2 0.3 fusion.6
  27.3 0.3 copy-done.1
  27.6 0.3 fusion.148
  27.9 0.5 collective-permute-done.2
  28.5 1.6 %collective-permute-start.3 = (bf16[64,768]{1,0:T(8,128)(2,1)S(1)}, bf16[64,768]{1,0:T(8,128)(2,1)S(1)}, u32[]{:S(2)}, u32[]{:S(2)}) collective-permute-start(bf16[64,768]{1,0:T(8,128)(2,1)S(1)} %add_convert_fusion.1), channel_id=1, source_target_pairs={{0,2},{1,3},{2,0},{3,1},{4,6},{5,7},{6,4},{7,5},{8,10},{9,11},{10,... | collective-permute-start | bytes 294920 | tf_op jit(solution)/shard_map/ppermute | solution.py:55
  30.1 3.3 %collective-permute-done.3 = bf16[64,768]{1,0:T(8,128)(2,1)S(1)} collective-permute-done((bf16[64,768]{1,0:T(8,128)(2,1)S(1)}, bf16[64,768]{1,0:T(8,128)(2,1)S(1)}, u32[]{:S(2)}, u32[]{:S(2)}) %collective-permute-start.3) | collective-permute-done | bytes 98336 | tf_op jit(solution)/shard_map/ppermute | solution.py:55
  33.8 1.1 %collective-permute-done.4 = f32[64,768]{1,0:T(8,128)S(1)} collective-permute-done((f32[64,768]{1,0:T(8,128)S(1)}, f32[64,768]{1,0:T(8,128)S(1)}, u32[]{:S(2)}, u32[]{:S(2)}) %collective-permute-start.4) | collective-permute-done | bytes 196640 | tf_op jit(solution)/shard_map/ppermute | solution.py:55
  35.4 0.3 convolution_convert_fusion.6
  36.2 0.3 fusion.7
  37.5 0.9 %collective-permute-done.5 = bf16[64,768]{1,0:T(8,128)(2,1)S(1)} collective-permute-done((bf16[64,768]{1,0:T(8,128)(2,1)S(1)}, bf16[64,768]{1,0:T(8,128)(2,1)S(1)}, u32[]{:S(2)}, u32[]{:S(2)}) %collective-permute-start.5) | collective-permute-done | bytes 98336 | tf_op jit(solution)/shard_map/ppermute | solution.py:55
  38.4 1.6 %collective-permute-start.6 = (bf16[64,768]{1,0:T(8,128)(2,1)S(1)}, bf16[64,768]{1,0:T(8,128)(2,1)S(1)}, u32[]{:S(2)}, u32[]{:S(2)}) collective-permute-start(bf16[64,768]{1,0:T(8,128)(2,1)S(1)} %add_convert_fusion), channel_id=1, source_target_pairs={{0,2},{1,3},{2,0},{3,1},{4,6},{5,7},{6,4},{7,5},{8,10},{9,11},{10,... | collective-permute-start | bytes 294920 | tf_op jit(solution)/shard_map/ppermute | solution.py:55
  40.2 3.1 %collective-permute-done.6 = bf16[64,768]{1,0:T(8,128)(2,1)S(1)} collective-permute-done((bf16[64,768]{1,0:T(8,128)(2,1)S(1)}, bf16[64,768]{1,0:T(8,128)(2,1)S(1)}, u32[]{:S(2)}, u32[]{:S(2)}) %collective-permute-start.6) | collective-permute-done | bytes 98336 | tf_op jit(solution)/shard_map/ppermute | solution.py:55
  43.6 1.3 %collective-permute-done.7 = f32[64,768]{1,0:T(8,128)S(1)} collective-permute-done((f32[64,768]{1,0:T(8,128)S(1)}, f32[64,768]{1,0:T(8,128)S(1)}, u32[]{:S(2)}, u32[]{:S(2)}) %collective-permute-start.7) | collective-permute-done | bytes 196640 | tf_op jit(solution)/shard_map/ppermute | solution.py:55
  45.3 1.4 %convolution_convert_fusion.1 = bf16[128,768]{1,0:T(8,128)(2,1)S(1)} fusion(bf16[768,768]{1,0:T(8,128)(2,1)S(1)} %copy-done, bf16[768,768]{1,0:T(8,128)(2,1)S(1)} %copy-done.6, f32[128,768]{1,0:T(8,128)S(1)} %get-tuple-element.6, f32[768]{0:T(1024)S(1)} %copy-done.11, f32[128]{0:T(128)S(1)} %add_rsqrt_fusion.1, f32[128]{0:T(128)S(1)} %broadcast_multiply_fusion.1), kind=kOutput, calls=%fused_computation.7 | convolution fusion | flops 308871168 | bytes 2953216 | tf_op jit(solution)/shard_map/dot_general | solution.py:171
  47.4 1.2 %collective-permute-done.8 = bf16[128,2,192]{2,0,1:T(8,128)(2,1)S(1)} collective-permute-done((bf16[128,2,192]{2,0,1:T(8,128)(2,1)S(1)}, bf16[128,2,192]{2,0,1:T(8,128)(2,1)S(1)}, u32[]{:S(2)}, u32[]{:S(2)}) %collective-permute-start.8) | collective-permute-done | bytes 98336 | tf_op jit(solution)/shard_map/ppermute | solution.py:55
  48.7 1.6 %collective-permute-start.9 = (f32[128,192]{1,0:T(8,128)S(1)}, f32[128,192]{1,0:T(8,128)S(1)}, u32[]{:S(2)}, u32[]{:S(2)}) collective-permute-start(f32[128,192]{1,0:T(8,128)S(1)} %select_bitcast_fusion), channel_id=1, source_target_pairs={{0,2},{1,3},{2,0},{3,1},{4,6},{5,7},{6,4},{7,5},{8,10},{9,11},{10,... | collective-permute-start | bytes 294920 | tf_op jit(solution)/shard_map/ppermute | solution.py:55
  50.3 4.1 %collective-permute-done.9 = f32[128,192]{1,0:T(8,128)S(1)} collective-permute-done((f32[128,192]{1,0:T(8,128)S(1)}, f32[128,192]{1,0:T(8,128)S(1)}, u32[]{:S(2)}, u32[]{:S(2)}) %collective-permute-start.9) | collective-permute-done | bytes 98336 | tf_op jit(solution)/shard_map/ppermute | solution.py:55
  55.0 3.8 %collective-permute-start.12 = (bf16[1,6272]{1,0:T(2,128)(2,1)S(1)}, bf16[1,6272]{1,0:T(2,128)(2,1)S(1)}, u32[]{:S(2)}, u32[]{:S(2)}) collective-permute-start(bf16[1,6272]{1,0:T(2,128)(2,1)S(1)} %get-tuple-element.21), channel_id=1, source_target_pairs={{0,12},{4,8},{8,4},{12,0},{1,13},{5,9},{9,5},{13,1},{2,14},{6,10},... | collective-permute-start | bytes 37640 | tf_op jit(solution)/shard_map/ppermute | solution.py:29
  58.8 0.7 %collective-permute-start.10 = (bf16[1,6272]{1,0:T(2,128)(2,1)S(1)}, bf16[1,6272]{1,0:T(2,128)(2,1)S(1)}, u32[]{:S(2)}, u32[]{:S(2)}) collective-permute-start(bf16[1,6272]{1,0:T(2,128)(2,1)S(1)} %get-tuple-element.23), channel_id=1, source_target_pairs={{0,4},{4,0},{8,12},{12,8},{1,5},{5,1},{9,13},{13,9},{2,6},{6,2},{1... | collective-permute-start | bytes 37640 | tf_op jit(solution)/shard_map/ppermute | solution.py:29
  59.5 1.3 %collective-permute-done.12 = bf16[1,6272]{1,0:T(2,128)(2,1)S(1)} collective-permute-done((bf16[1,6272]{1,0:T(2,128)(2,1)S(1)}, bf16[1,6272]{1,0:T(2,128)(2,1)S(1)}, u32[]{:S(2)}, u32[]{:S(2)}) %collective-permute-start.12) | collective-permute-done | bytes 12576 | tf_op jit(solution)/shard_map/ppermute | solution.py:29
  60.8 2.7 %collective-permute-done.11 = bf16[1,6272]{1,0:T(2,128)(2,1)S(1)} collective-permute-done((bf16[1,6272]{1,0:T(2,128)(2,1)S(1)}, bf16[1,6272]{1,0:T(2,128)(2,1)S(1)}, u32[]{:S(2)}, u32[]{:S(2)}) %collective-permute-start.11) | collective-permute-done | bytes 12576 | tf_op jit(solution)/shard_map/ppermute | solution.py:29
  63.7 0.6 gather_fusion.1
  65.1 0.6 copy.47
  (122 shorter events, 8.7 us)
Async XLA Ops:
  0.0 45.3 %copy-start = (bf16[768,768]{1,0:T(8,128)(2,1)S(1)}, bf16[768,768]{1,0:T(8,128)(2,1)}, u32[]{:S(2)}) copy-start(bf16[768,768]{1,0:T(8,128)(2,1)} %param.27) | copy-start | bytes 3538948
  17.5 1.3 %collective-permute-start = (bf16[4,32,192]{2,1,0:T(8,128)(2,1)S(1)}, bf16[4,32,192]{2,1,0:T(8,128)(2,1)S(1)}, u32[]{:S(2)}, u32[]{:S(2)}) collective-permute-start(bf16[4,32,192]{2,1,0:T(8,128)(2,1)S(1)} %broadcast_select_fusion.6), channel_id=1, source_target_pairs={{0,1},{1,0},{2,3},{3,2},{4,5},{5,4},{6,7},{7,6},{8,9},{9,8},{10,11... | collective-permute-start | bytes 147464 | tf_op jit(solution)/shard_map/ppermute | solution.py:55
  18.9 5.1 %collective-permute-start.1 = (bf16[4,32,384]{2,1,0:T(8,128)(2,1)S(1)}, bf16[4,32,384]{2,1,0:T(8,128)(2,1)S(1)}, u32[]{:S(2)}, u32[]{:S(2)}) collective-permute-start(bf16[4,32,384]{2,1,0:T(8,128)(2,1)S(1)} %maximum_select_fusion.3), channel_id=1, source_target_pairs={{0,2},{1,3},{2,0},{3,1},{4,6},{5,7},{6,4},{7,5},{8,10},{9,11},{10,... | collective-permute-start | bytes 294920 | tf_op jit(solution)/shard_map/ppermute | solution.py:55
  20.6 4.3 %copy-start.7 = (bf16[3,768,192]{1,2,0:T(8,128)(2,1)S(1)}, bf16[3,768,192]{1,2,0:T(8,128)(2,1)}, u32[]{:S(2)}) copy-start(bf16[3,768,192]{1,2,0:T(8,128)(2,1)} %param.21) | copy-start | bytes 2654212
  20.6 4.3 %copy-start.9 = (f32[768]{0:T(1024)S(1)}, f32[768]{0:T(1024)}, u32[]{:S(2)}) copy-start(f32[768]{0:T(1024)} %param.17) | copy-start | bytes 9220
  25.9 1.0 %copy-start.2 = (bf16[192,768]{1,0:T(8,128)(2,1)S(1)}, bf16[192,768]{1,0:T(8,128)(2,1)}, u32[]{:S(2)}) copy-start(bf16[192,768]{1,0:T(8,128)(2,1)} %param.22) | copy-start | bytes 884740
  26.2 1.0 %copy-start.4 = (f32[768]{0:T(1024)S(1)}, f32[768]{0:T(1024)}, u32[]{:S(2)}) copy-start(f32[768]{0:T(1024)} %param.19) | copy-start | bytes 9220
  26.5 1.1 %copy-start.1 = (bf16[2,768,192]{1,2,0:T(8,128)(2,1)S(1)}, bf16[2,768,192]{1,2,0:T(8,128)(2,1)}, u32[]{:S(2)}) copy-start(bf16[2,768,192]{1,2,0:T(8,128)(2,1)} %param.24) | copy-start | bytes 1769476
  27.1 1.4 %collective-permute-start.2 = (bf16[64,768]{1,0:T(8,128)(2,1)S(1)}, bf16[64,768]{1,0:T(8,128)(2,1)S(1)}, u32[]{:S(2)}, u32[]{:S(2)}) collective-permute-start(bf16[64,768]{1,0:T(8,128)(2,1)S(1)} %broadcast_select_fusion.5), channel_id=1, source_target_pairs={{0,1},{1,0},{2,3},{3,2},{4,5},{5,4},{6,7},{7,6},{8,9},{9,8},{10,11... | collective-permute-start | bytes 294920 | tf_op jit(solution)/shard_map/ppermute | solution.py:55
  28.5 4.9 %collective-permute-start.3 = (bf16[64,768]{1,0:T(8,128)(2,1)S(1)}, bf16[64,768]{1,0:T(8,128)(2,1)S(1)}, u32[]{:S(2)}, u32[]{:S(2)}) collective-permute-start(bf16[64,768]{1,0:T(8,128)(2,1)S(1)} %add_convert_fusion.1), channel_id=1, source_target_pairs={{0,2},{1,3},{2,0},{3,1},{4,6},{5,7},{6,4},{7,5},{8,10},{9,11},{10,... | collective-permute-start | bytes 294920 | tf_op jit(solution)/shard_map/ppermute | solution.py:55
  33.4 1.5 %collective-permute-start.4 = (f32[64,768]{1,0:T(8,128)S(1)}, f32[64,768]{1,0:T(8,128)S(1)}, u32[]{:S(2)}, u32[]{:S(2)}) collective-permute-start(f32[64,768]{1,0:T(8,128)S(1)} %convert_add_fusion.3), channel_id=1, source_target_pairs={{0,1},{1,0},{2,3},{3,2},{4,5},{5,4},{6,7},{7,6},{8,9},{9,8},{10,11... | collective-permute-start | bytes 589832 | tf_op jit(solution)/shard_map/ppermute | solution.py:55
  33.5 1.8 %copy-start.8 = (bf16[768,192]{0,1:T(8,128)(2,1)S(1)}, bf16[768,192]{0,1:T(8,128)(2,1)}, u32[]{:S(2)}) copy-start(bf16[768,192]{0,1:T(8,128)(2,1)} %param.23) | copy-start | bytes 884740
  33.5 1.8 %copy-start.10 = (f32[768]{0:T(1024)S(1)}, f32[768]{0:T(1024)}, u32[]{:S(2)}) copy-start(f32[768]{0:T(1024)} %param.18) | copy-start | bytes 9220
  35.8 1.0 %copy-start.3 = (bf16[192,768]{1,0:T(8,128)(2,1)S(1)}, bf16[192,768]{1,0:T(8,128)(2,1)}, u32[]{:S(2)}) copy-start(bf16[192,768]{1,0:T(8,128)(2,1)} %param.25) | copy-start | bytes 884740
  36.2 1.1 %copy-start.5 = (f32[2,64]{1,0:T(2,128)S(1)}, f32[2,64]{1,0:T(2,128)}, u32[]{:S(2)}) copy-start(f32[2,64]{1,0:T(2,128)} %param.16) | copy-start | bytes 1540
  37.0 1.4 %collective-permute-start.5 = (bf16[64,768]{1,0:T(8,128)(2,1)S(1)}, bf16[64,768]{1,0:T(8,128)(2,1)S(1)}, u32[]{:S(2)}, u32[]{:S(2)}) collective-permute-start(bf16[64,768]{1,0:T(8,128)(2,1)S(1)} %broadcast_select_fusion.2), channel_id=1, source_target_pairs={{0,1},{1,0},{2,3},{3,2},{4,5},{5,4},{6,7},{7,6},{8,9},{9,8},{10,11... | collective-permute-start | bytes 294920 | tf_op jit(solution)/shard_map/ppermute | solution.py:55
  38.4 4.9 %collective-permute-start.6 = (bf16[64,768]{1,0:T(8,128)(2,1)S(1)}, bf16[64,768]{1,0:T(8,128)(2,1)S(1)}, u32[]{:S(2)}, u32[]{:S(2)}) collective-permute-start(bf16[64,768]{1,0:T(8,128)(2,1)S(1)} %add_convert_fusion), channel_id=1, source_target_pairs={{0,2},{1,3},{2,0},{3,1},{4,6},{5,7},{6,4},{7,5},{8,10},{9,11},{10,... | collective-permute-start | bytes 294920 | tf_op jit(solution)/shard_map/ppermute | solution.py:55
  43.4 1.5 %collective-permute-start.7 = (f32[64,768]{1,0:T(8,128)S(1)}, f32[64,768]{1,0:T(8,128)S(1)}, u32[]{:S(2)}, u32[]{:S(2)}) collective-permute-start(f32[64,768]{1,0:T(8,128)S(1)} %convert_add_fusion.2), channel_id=1, source_target_pairs={{0,1},{1,0},{2,3},{3,2},{4,5},{5,4},{6,7},{7,6},{8,9},{9,8},{10,11... | collective-permute-start | bytes 589832 | tf_op jit(solution)/shard_map/ppermute | solution.py:55
  43.6 1.7 %copy-start.6 = (bf16[768,768]{1,0:T(8,128)(2,1)S(1)}, bf16[768,768]{1,0:T(8,128)(2,1)}, u32[]{:S(2)}) copy-start(bf16[768,768]{1,0:T(8,128)(2,1)} %param.26) | copy-start | bytes 3538948
  43.6 1.7 %copy-start.11 = (f32[768]{0:T(1024)S(1)}, f32[768]{0:T(1024)}, u32[]{:S(2)}) copy-start(f32[768]{0:T(1024)} %param.20) | copy-start | bytes 9220
  47.2 1.4 %collective-permute-start.8 = (bf16[128,2,192]{2,0,1:T(8,128)(2,1)S(1)}, bf16[128,2,192]{2,0,1:T(8,128)(2,1)S(1)}, u32[]{:S(2)}, u32[]{:S(2)}) collective-permute-start(bf16[128,2,192]{2,0,1:T(8,128)(2,1)S(1)} %select_bitcast_fusion.1), channel_id=1, source_target_pairs={{0,1},{1,0},{2,3},{3,2},{4,5},{5,4},{6,7},{7,6},{8,9},{9,8},{10,11... | collective-permute-start | bytes 294920 | tf_op jit(solution)/shard_map/ppermute | solution.py:55
  48.7 5.6 %collective-permute-start.9 = (f32[128,192]{1,0:T(8,128)S(1)}, f32[128,192]{1,0:T(8,128)S(1)}, u32[]{:S(2)}, u32[]{:S(2)}) collective-permute-start(f32[128,192]{1,0:T(8,128)S(1)} %select_bitcast_fusion), channel_id=1, source_target_pairs={{0,2},{1,3},{2,0},{3,1},{4,6},{5,7},{6,4},{7,5},{8,10},{9,11},{10,... | collective-permute-start | bytes 294920 | tf_op jit(solution)/shard_map/ppermute | solution.py:55
  55.0 5.8 %collective-permute-start.12 = (bf16[1,6272]{1,0:T(2,128)(2,1)S(1)}, bf16[1,6272]{1,0:T(2,128)(2,1)S(1)}, u32[]{:S(2)}, u32[]{:S(2)}) collective-permute-start(bf16[1,6272]{1,0:T(2,128)(2,1)S(1)} %get-tuple-element.21), channel_id=1, source_target_pairs={{0,12},{4,8},{8,4},{12,0},{1,13},{5,9},{9,5},{13,1},{2,14},{6,10},... | collective-permute-start | bytes 37640 | tf_op jit(solution)/shard_map/ppermute | solution.py:29
  58.8 4.7 %collective-permute-start.11 = (bf16[1,6272]{1,0:T(2,128)(2,1)S(1)}, bf16[1,6272]{1,0:T(2,128)(2,1)S(1)}, u32[]{:S(2)}, u32[]{:S(2)}) collective-permute-start(bf16[1,6272]{1,0:T(2,128)(2,1)S(1)} %get-tuple-element.22), channel_id=1, source_target_pairs={{0,8},{4,12},{8,0},{12,4},{1,9},{5,13},{9,1},{13,5},{2,10},{6,14},... | collective-permute-start | bytes 37640 | tf_op jit(solution)/shard_map/ppermute | solution.py:29
  58.8 4.7 %collective-permute-start.10 = (bf16[1,6272]{1,0:T(2,128)(2,1)S(1)}, bf16[1,6272]{1,0:T(2,128)(2,1)S(1)}, u32[]{:S(2)}, u32[]{:S(2)}) collective-permute-start(bf16[1,6272]{1,0:T(2,128)(2,1)S(1)} %get-tuple-element.23), channel_id=1, source_target_pairs={{0,4},{4,0},{8,12},{12,8},{1,5},{5,1},{9,13},{13,9},{2,6},{6,2},{1... | collective-permute-start | bytes 37640 | tf_op jit(solution)/shard_map/ppermute | solution.py:29
